TPU v7x, 256 devices: a whole 4x4x8 slice. The times are simulated.
256 devices in a mesh: path: 64 (over z, x, core), rep: 4 (over y).
Axes of the slice: x: 4, y: 4, z: 8, core: 2. Of those that a mesh axis runs over, the one named last changes fastest.
Arguments:
- start_state: float32 [32, 65536], P(None, 'path'), may hold values from -1.8 to 1.8
- increments: float32 [2, 32, 65536], P(None, None, 'path'), may hold values from -6 to 6
- vol_factor: float32 [32, 32], replicated, may hold values from -0.3 to 0.3
- quad_dirs: float32 [223, 32], replicated, may hold values from -1.5 to 1.5
- bundle_ids: int32 [2, 65536, 1], P(None, 'path'), may hold values from 0 to 255; in each aligned block of 1024 rows (0 to 1023, 1024 to 2047, ..., all dimensions but the last counted through in order) at most 8 rows name the same one
- bundle_slot: int32 [256], replicated, may hold values from 0 to 255, each once
Outputs:
- values: float32 [2, 65536], P(None, 'path')
- coefficients: float32 [2, 256, 256], P(None, 'path', 'rep')
Inputs may be any that keep to these rules, and one draw needn't show every extreme that they name: `bundle_ids`: at each date, no bundle id appears more than 8 times among the paths of one device; in every draw some device holds exactly 8 paths of one bundle. A permutation: bundle b sits at slot bundle_slot[b], and slot s belongs to the owner s // 4 along path.
All inputs are finite; a program needn't handle non-finite values.
Results may differ from a plain program's by a relative error of at most 0.0003.
Values sent between devices are 32-bit elements; how exact they have to be, the bound alone decides.
No kernel may reach another device: no remote copies, remote signals or barrier semaphores. Data moves between devices by JAX's collectives and lax.ppermute only.
A program may use at most 64 MiB of HBM per device.

v0:
```python
import jax
import jax.numpy as jnp
from jax import lax
from jax.sharding import PartitionSpec as P

BASIS = 256
RIDGE_TERM = 32.0
DISCOUNT = 0.97
NOTIONAL = 10.0
HIGHEST = lax.Precision.HIGHEST


def basis_features(states, quad_dirs):
    projected = jnp.dot(quad_dirs, states, precision=HIGHEST, preferred_element_type=jnp.float32)
    constant = jnp.ones((1, states.shape[1]), jnp.float32)
    return jnp.concatenate([constant, states, projected * projected], axis=0)


def moment_features(states, quad_dirs, offsets):
    projected = jnp.dot(quad_dirs, states, precision=HIGHEST, preferred_element_type=jnp.float32)
    constant = jnp.ones((1, states.shape[1]), jnp.float32)
    return jnp.concatenate([constant, states, projected * projected + offsets[:, None]], axis=0)


def exercise_value(states):
    return NOTIONAL * jnp.maximum(jnp.mean(jnp.exp(states), axis=0) - 1.0, 0.0)


def backward_period(bundle_of, state_now, state_next, value_next, bundle_slot, quad_dirs, offsets):
    path_count = state_now.shape[1]
    bundles = bundle_slot.shape[0]
    owners = lax.axis_size("path")
    per_owner = bundles // owners
    capacity = max(2, 2 * path_count // bundles)
    column_count = BASIS // lax.axis_size("rep")
    rep_index = lax.axis_index("rep")
    share_count = 1
    share_slots = -(-capacity // share_count)
    padded_capacity = share_slots * share_count
    owner_block = per_owner * share_slots
    slot_of = jnp.take(bundle_slot, bundle_of)
    ranking = jnp.argsort(slot_of, stable=True)
    ordered = jnp.take(slot_of, ranking)
    group_start = jnp.searchsorted(ordered, ordered, side="left")
    rank_within = jnp.arange(path_count, dtype=jnp.int32) - group_start
    position = ordered * padded_capacity + rank_within
    regress_rows = jnp.concatenate(
        [basis_features(state_next, quad_dirs), value_next[None, :]], axis=0
    )
    row_count = regress_rows.shape[0]
    outgoing = jnp.zeros((row_count, bundles * padded_capacity), jnp.float32)
    outgoing = outgoing.at[:, position].set(jnp.take(regress_rows, ranking, axis=1))
    outgoing = outgoing.reshape(row_count, bundles, share_slots, share_count)
    outgoing = outgoing.reshape(row_count, owners, owner_block)
    arrived = lax.all_to_all(outgoing, "path", split_axis=1, concat_axis=1, tiled=True)
    arrived = arrived.reshape(row_count, owners * owner_block)
    features = arrived[:BASIS]
    target = arrived[BASIS]
    features = features.reshape(BASIS, owners, per_owner, share_slots)
    target = target.reshape(owners, per_owner, share_slots)
    column_block = lax.dynamic_slice_in_dim(features, rep_index * column_count, column_count, 0)
    gram_part = jnp.einsum("ksbm,csbm->bkc", features, column_block, precision=HIGHEST)
    gram_matrix = lax.all_gather(gram_part, "rep", axis=2, tiled=True)
    right_side = jnp.einsum("ksbm,sbm->bk", features, target, precision=HIGHEST)
    gram_matrix = gram_matrix + RIDGE_TERM * jnp.eye(BASIS, dtype=jnp.float32)
    factor = jnp.linalg.cholesky(gram_matrix)
    halfway = lax.linalg.triangular_solve(
        factor, right_side[:, :, None], left_side=True, lower=True
    )
    weights = lax.linalg.triangular_solve(
        factor, halfway, left_side=True, lower=True, transpose_a=True
    )[:, :, 0]
    weight_block = lax.dynamic_slice_in_dim(weights, rep_index * column_count, column_count, 1)
    weight_table = lax.all_gather(weight_block, "path", axis=0, tiled=True)
    picked = jnp.take(weight_table, slot_of, axis=0)
    moments = moment_features(state_now, quad_dirs, offsets)
    moment_block = lax.dynamic_slice_in_dim(moments, rep_index * column_count, column_count, 0)
    partial_terms = jnp.sum(picked.T * moment_block, axis=0)
    carried = lax.psum(partial_terms, "rep")
    value_now = jnp.maximum(exercise_value(state_now), DISCOUNT * carried)
    return (value_now, weight_block)


def body(start_state, increments, vol_factor, quad_dirs, bundle_ids, bundle_slot):
    middle = start_state + jnp.dot(
        vol_factor, increments[0], precision=HIGHEST, preferred_element_type=jnp.float32
    )
    final = middle + jnp.dot(
        vol_factor, increments[1], precision=HIGHEST, preferred_element_type=jnp.float32
    )
    mixed = jnp.dot(quad_dirs, vol_factor, precision=HIGHEST, preferred_element_type=jnp.float32)
    offsets = jnp.sum(mixed * mixed, axis=1)
    value_final = exercise_value(final)
    value_middle, weights_middle = backward_period(
        bundle_ids[0, :, 0], middle, final, value_final, bundle_slot, quad_dirs, offsets
    )
    value_start, weights_start = backward_period(
        bundle_ids[1, :, 0], start_state, middle, value_middle, bundle_slot, quad_dirs, offsets
    )
    return (jnp.stack([value_middle, value_start]), jnp.stack([weights_middle, weights_start]))


def solution(mesh):
    placed = (P(None, "path"), P(None, None, "path"), P(), P(), P(None, "path", None), P())
    return jax.shard_map(
        body,
        mesh=mesh,
        in_specs=placed,
        out_specs=(P(None, "path"), P(None, "path", "rep")),
        check_vma=False,
    )
```

profile of v0, /device:TPU:1, one launch (start us, length us, event | category | flops | bytes accessed | tf_op | source)
XLA Modules:
  0.0 985.5 jit_solution(9080812871805606301)
XLA Ops:
  7.9 6.9 gather_fusion.2
  24.3 50.7 %while.47 = (s32[]{:T(128)}, u32[1024]{0:T(1024)S(1)}, u32[1024]{0:T(1024)S(1)}, s32[1024]{0:T(1024)S(1)}, s32[]{:T(128)}, /*index=5*/s32[]{:T(128)}, s32[]{}) while((s32[]{:T(128)}, u32[1024]{0:T(1024)S(1)}, u32[1024]{0:T(1024)S(1)}, s32[1024]{0:T(1024)S(1)}, s32[]{:T(128)}, /*index=5*/s32[]{:T(128)}, s32[]{}) %tuple.133), condition=%wide.region_3.0_spmd.clone, body=%wide.region_2.5_spmd.clone.sunk | while | flops 19460 | bytes 67685 | solution.py:44
  75.1 6.9 gather_fusion.5
  92.7 50.7 %while.48 = (s32[]{:T(128)}, u32[1024]{0:T(1024)S(1)}, u32[1024]{0:T(1024)S(1)}, s32[1024]{0:T(1024)S(1)}, s32[]{:T(128)}, /*index=5*/s32[]{:T(128)}, s32[]{}) while((s32[]{:T(128)}, u32[1024]{0:T(1024)S(1)}, u32[1024]{0:T(1024)S(1)}, s32[1024]{0:T(1024)S(1)}, s32[]{:T(128)}, /*index=5*/s32[]{:T(128)}, s32[]{}) %tuple.130), condition=%wide.region_16.24_spmd.clone, body=%wide.region_15.23_spmd.clone.sunk | while | flops 19460 | bytes 67685 | solution.py:44
  146.8 10.5 %scatter_custom_fusion = f32[257,2048]{0,1:T(8,128)} fusion(s32[1024]{0:T(1024)S(1)} %get-tuple-element.286, f32[]{:T(128)} %constant.182.clone.1, f32[]{:T(128)} %constant.164.clone.2, pred[1024]{0:T(1024)(128)(4,1)S(1)} %get-tuple-element.260, f32[257,1024]{0,1:T(8,128)S(1)} %copy.82, s32[1024]{0:T(1024)S(1)} %fusion.64), kind=kCustom, calls=%fused_computation.30 | custom fusion | flops 263168 | bytes 3683336 | tf_op jit(solution)/shard_map/scatter | solution.py:52
  157.2 13.0 %all-to-all-start = ((f32[257,64,32]{0,2,1:T(8,128)}), f32[257,64,32]{0,2,1:T(8,128)S(1)}, u32[]{:S(2)}, u32[]{:S(2)}) async-start(f32[257,64,32]{0,2,1:T(8,128)} %bitcast.257), calls=%async_computation | async-start | bytes 6291456 | tf_op jit(solution)/shard_map/all_to_all | solution.py:55
  170.5 72.2 %all-to-all-done = f32[257,64,32]{0,2,1:T(8,128)S(1)} async-done(((f32[257,64,32]{0,2,1:T(8,128)}), f32[257,64,32]{0,2,1:T(8,128)S(1)}, u32[]{:S(2)}, u32[]{:S(2)}) %all-to-all-start) | async-done | bytes 2105376 | tf_op jit(solution)/shard_map/all_to_all | solution.py:55
  261.6 6.0 fusion.78
  268.2 8.3 all-gather.5.cloned.1.call-done
  279.2 47.3 %custom-call.25 = f32[4,128,128]{2,1,0:T(8,128)S(1)} custom-call(f32[4,128,128]{2,1,0:T(8,128)S(1)} %cholesky.198), custom_call_target="Cholesky" | custom-call | tf_op jit(solution)/shard_map/jit(cholesky)/cholesky | solution.py:66
  326.7 39.3 %custom-call.26 = f32[4,1,128,128]{2,3,1,0:T(8,128)S(1)} custom-call(f32[4,1,128,128]{3,2,1,0:T(8,128)S(1)} %select_bitcast_fusion.1), custom_call_target="InvertDiagBlocksLowerTriangular" | custom-call | tf_op jit(solution)/shard_map/jit(cholesky)/cholesky | solution.py:66
  367.1 46.9 %custom-call.27 = f32[4,128,128]{2,1,0:T(8,128)S(1)} custom-call(f32[4,128,128]{2,1,0:T(8,128)S(1)} %convolution_subtract_fusion.1), custom_call_target="Cholesky" | custom-call | tf_op jit(solution)/shard_map/jit(cholesky)/cholesky | solution.py:66
  419.4 78.8 %custom-call.29 = f32[4,2,128,128]{2,3,1,0:T(8,128)S(1)} custom-call(f32[4,2,128,128]{3,2,1,0:T(8,128)S(1)} %bitcast.260), custom_call_target="InvertDiagBlocksLowerTriangular" | custom-call | tf_op jit(solution)/shard_map/triangular_solve/custom-call.4 | solution.py:70
  500.9 53.3 %all-gather = f32[256,64,1]{1,2,0:T(1,128)S(1)} all-gather(f32[4,64,1]{1,2,0:T(1,128)S(1)} %fusion.70), channel_id=2, replica_groups=mesh['path'=64,'rep'=4] {'path'}, dimensions={0}, use_global_device_ids=true | all-gather | bytes 66560 | tf_op jit(solution)/shard_map/all_gather | solution.py:74
  557.4 7.2 psum.14
  565.5 10.6 %scatter_custom_fusion.1 = f32[257,2048]{0,1:T(8,128)} fusion(s32[1024]{0:T(1024)} %get-tuple-element.285, f32[]{:T(128)} %constant.182.clone.1, f32[]{:T(128)} %constant.164.clone.2, pred[1024]{0:T(1024)(128)(4,1)S(1)} %copy-done.26, f32[257,1024]{0,1:T(8,128)S(1)} %copy.92, s32[1024]{0:T(1024)S(1)} %copy-done.14), kind=kCustom, calls=%fused_computation.28 | custom fusion | flops 263168 | bytes 3164160 | tf_op jit(solution)/shard_map/scatter | solution.py:52
  576.1 82.5 %all_to_all.10 = f32[257,64,32]{0,2,1:T(8,128)S(1)} all-to-all(f32[257,64,32]{0,2,1:T(8,128)} %bitcast.258), channel_id=1, replica_groups=mesh['path'=64,'rep'=4] {'path'}, dimensions={1} | all-to-all | bytes 4210688 | tf_op jit(solution)/shard_map/all_to_all | solution.py:55
  677.9 5.9 fusion.79
  692.3 47.1 %custom-call.30 = f32[4,128,128]{2,1,0:T(8,128)S(1)} custom-call(f32[4,128,128]{2,1,0:T(8,128)S(1)} %cholesky.201), custom_call_target="Cholesky" | custom-call | tf_op jit(solution)/shard_map/jit(cholesky)/cholesky | solution.py:66
  739.6 39.3 %custom-call.31 = f32[4,1,128,128]{2,3,1,0:T(8,128)S(1)} custom-call(f32[4,1,128,128]{3,2,1,0:T(8,128)S(1)} %select_bitcast_fusion), custom_call_target="InvertDiagBlocksLowerTriangular" | custom-call | tf_op jit(solution)/shard_map/jit(cholesky)/cholesky | solution.py:66
  780.0 46.9 %custom-call.32 = f32[4,128,128]{2,1,0:T(8,128)S(1)} custom-call(f32[4,128,128]{2,1,0:T(8,128)S(1)} %convolution_subtract_fusion), custom_call_target="Cholesky" | custom-call | tf_op jit(solution)/shard_map/jit(cholesky)/cholesky | solution.py:66
  831.6 78.9 %custom-call.34 = f32[4,2,128,128]{2,3,1,0:T(8,128)S(1)} custom-call(f32[4,2,128,128]{3,2,1,0:T(8,128)S(1)} %bitcast.259), custom_call_target="InvertDiagBlocksLowerTriangular" | custom-call | tf_op jit(solution)/shard_map/triangular_solve/custom-call.4 | solution.py:70
  913.2 53.3 %all-gather.1 = f32[256,64,1]{1,2,0:T(1,128)S(1)} all-gather(f32[4,64,1]{1,2,0:T(1,128)S(1)} %fusion.69), channel_id=3, replica_groups=mesh['path'=64,'rep'=4] {'path'}, dimensions={0}, use_global_device_ids=true | all-gather | bytes 66560 | tf_op jit(solution)/shard_map/all_gather | solution.py:74
  969.7 7.2 psum.15
  (304 shorter events, 208.9 us)
Async XLA Ops:
  7.2 137.4 %copy-start = (f32[223,32]{0,1:T(8,128)S(1)}, f32[223,32]{0,1:T(8,128)}, u32[]{:S(2)}) copy-start(f32[223,32]{0,1:T(8,128)} %param.26) | copy-start | bytes 85636
  92.6 50.7 %copy-start.9 = (f32[32,1024]{1,0:T(8,128)S(1)}, f32[32,1024]{1,0:T(8,128)}, u32[]{:S(2)}) copy-start(f32[32,1024]{1,0:T(8,128)} %param.23) | copy-start | bytes 393220
  92.6 50.7 %copy-start.11 = (f32[2,32,1024]{2,1,0:T(8,128)S(1)}, f32[2,32,1024]{2,1,0:T(8,128)}, u32[]{:S(2)}) copy-start(f32[2,32,1024]{2,1,0:T(8,128)} %param.24) | copy-start | bytes 786436
  92.7 50.7 %copy-start.12 = (f32[32,32]{1,0:T(8,128)S(1)}, f32[32,32]{1,0:T(8,128)}, u32[]{:S(2)}) copy-start(f32[32,32]{1,0:T(8,128)} %param.25) | copy-start | bytes 12292
  157.2 85.4 %all-to-all-start = ((f32[257,64,32]{0,2,1:T(8,128)}), f32[257,64,32]{0,2,1:T(8,128)S(1)}, u32[]{:S(2)}, u32[]{:S(2)}) async-start(f32[257,64,32]{0,2,1:T(8,128)} %bitcast.257), calls=%async_computation | async-start | bytes 6291456 | tf_op jit(solution)/shard_map/all_to_all | solution.py:55
  170.2 106.3 %all-gather.5.cloned.1.call-start = ((), (), s32[]{:S(2)}) async-start(), calls=%async_computation.2 | async-start | bytes 1310720 | tf_op jit(solution)/shard_map/all_gather | solution.py:63
  254.2 435.4 %all-gather.7.cloned.1.call-start = ((), (), s32[]{:S(2)}) async-start(), calls=%async_computation.3 | async-start | bytes 1310720 | tf_op jit(solution)/shard_map/all_gather | solution.py:63
  367.1 47.4 %copy-start.31 = (s32[2]{0:T(128)S(1)}, s32[2]{0:T(128)}, u32[]{:S(2)}) copy-start(s32[2]{0:T(128)} %iota_multiply_fusion) | copy-start | bytes 28
  414.6 83.6 %copy-start.23 = (f32[4,128,1]{1,0,2:T(4,128)S(1)}, f32[4,128,1]{1,0,2:T(4,128)}, u32[]{:S(2)}) copy-start(f32[4,128,1]{1,0,2:T(4,128)} %slice.172) | copy-start | bytes 6148
  500.9 53.3 %copy-start.15 = (f32[4,64,1]{1,2,0:T(1,128)}, f32[4,64,1]{1,2,0:T(1,128)S(1)}, u32[]{:S(2)}) copy-start(f32[4,64,1]{1,2,0:T(1,128)S(1)} %fusion.70) | copy-start | bytes 3076
  554.2 3.1 copy-start.5
  554.2 3.1 copy-start.8
  554.2 3.1 copy-start.28
  557.0 7.6 copy-start.17
  557.0 7.6 copy-start.4
  665.0 7.3 copy-start.25
  827.4 83.1 %copy-start.22 = (f32[4,128,1]{1,0,2:T(4,128)S(1)}, f32[4,128,1]{1,0,2:T(4,128)}, u32[]{:S(2)}) copy-start(f32[4,128,1]{1,0,2:T(4,128)} %slice.179) | copy-start | bytes 6148
  827.6 83.8 %copy-start.20 = (f32[4,1,256,1]{2,0,1,3:T(4,128)S(1)}, f32[4,1,256,1]{2,0,1,3:T(4,128)}, u32[]{:S(2)}) copy-start(f32[4,1,256,1]{2,0,1,3:T(4,128)} %copy-done.19) | copy-start | bytes 12292
  831.5 134.9 %copy-start.21 = (s32[1024]{0:T(1024)S(1)}, s32[1024]{0:T(1024)}, u32[]{:S(2)}) copy-start(s32[1024]{0:T(1024)} %fusion.68) | copy-start | bytes 12292
  966.4 3.1 copy-start.6
  966.4 3.1 copy-start.10
  966.5 3.1 copy-start.27
  969.3 7.6 copy-start.18
  969.3 8.2 copy-start.16
  (11 other events, 8.8 us)
Sparse Core Ops, SparseCore 0:
  254.3 22.1 all-gather.4
  670.2 19.2 all-gather.6
where the time goes:
time: 994 us; the launch traced here: 985 us
  other arithmetic  466 us (47%)
  blocking collectives  204 us (21%)
  local copies, waits for them, and re-layouts  163 us (16%)
  waiting for transfers between devices  85.1 us (9%)
  matrix products  37.5 us (4%)
  between operations  15.3 us (2%)
  starting transfers between devices  13.3 us (1%)
    another operation x18, other arithmetic, backward_period(): factor = jnp.linalg.cholesky(gram_matrix)  268 us
    another operation x10, other arithmetic, backward_period(): lax.linalg.triangular_solve(factor, halfway, left_side=True, lower=True,...  159 us
    all_gather x2, blocking collectives, backward_period(): weight_table = lax.all_gather(weight_block, 'path', axis=0, tiled=True)  107 us
    gather x22, local copies, waits for them, and re-layouts, backward_period(): group_start = jnp.searchsorted(ordered, ordered, side='left')  99.6 us
    all_to_all x1, blocking collectives, backward_period(): lax.all_to_all(outgoing, 'path', split_axis=1, concat_axis=1, tiled=True)  82.5 us
    all_to_all x1, waiting for transfers between devices, backward_period(): lax.all_to_all(outgoing, 'path', split_axis=1, concat_axis=1, tiled=True)  72.2 us
    scatter x2, other arithmetic, backward_period(): outgoing.at[:, position].set(jnp.take(regress_rows, ranking, axis=1))  21 us
  transfers between devices with their start and end apart: 3, of which 3 were waited for; matrix products, arithmetic and copies ran while one was open for 3% of the time, Pallas kernels for 0%

commit v1 on v0

--- a/solution.py
+++ b/solution.py
@@ -71,7 +71,9 @@
         factor, halfway, left_side=True, lower=True, transpose_a=True
     )[:, :, 0]
     weight_block = lax.dynamic_slice_in_dim(weights, rep_index * column_count, column_count, 1)
-    weight_table = lax.all_gather(weight_block, "path", axis=0, tiled=True)
+    weight_table = jnp.concatenate(
+        jax.lax.all_to_all(jnp.stack([weight_block] * jax.lax.psum(1, "path")), "path", 0, 0), 0
+    )
     picked = jnp.take(weight_table, slot_of, axis=0)
     moments = moment_features(state_now, quad_dirs, offsets)
     moment_block = lax.dynamic_slice_in_dim(moments, rep_index * column_count, column_count, 0)

time: 994 us -> 934 us (0.940)
  blocking collectives: 204 us -> 94.7 us
  starting transfers between devices: 13.3 us -> 38.8 us
  waiting for transfers between devices: 85.1 us -> 106 us
    all_gather x2 -> x0, blocking collectives: 107 us -> none  [backward_period(): weight_table = lax.all_gather(weight_block, 'path', axis=0, tiled=True)]
    all_to_all x0 -> x2, starting transfers between devices: none -> 25.5 us  [backward_period(): jax.lax.all_to_all(jnp.stack([weight_block] * jax.lax.psum(1, 'path')), '...]
    all_to_all x0 -> x2, waiting for transfers between devices: none -> 19.5 us  [backward_period(): jax.lax.all_to_all(jnp.stack([weight_block] * jax.lax.psum(1, 'path')), '...]
    another operation x10 -> x8, other arithmetic: 159 us -> 159 us  [backward_period(): lax.linalg.triangular_solve(factor, halfway, left_side=True, lower=True,...]
  transfers between devices with their start and end apart: 3 -> 5, of which waited for: 3 -> 5; matrix products, arithmetic and copies ran while one was open for 3% -> 3% of each run, Pallas kernels for 0% -> 0%
where the time goes in v1:
time: 934 us; the launch traced here: 926 us
  other arithmetic  467 us (50%)
  local copies, waits for them, and re-layouts  165 us (18%)
  waiting for transfers between devices  106 us (11%)
  blocking collectives  94.7 us (10%)
  starting transfers between devices  38.8 us (4%)
  matrix products  37.7 us (4%)
  between operations  15.1 us (2%)
    another operation x18, other arithmetic, backward_period(): factor = jnp.linalg.cholesky(gram_matrix)  268 us
    another operation x8, other arithmetic, backward_period(): lax.linalg.triangular_solve(factor, halfway, left_side=True, lower=True,...  159 us
    gather x22, local copies, waits for them, and re-layouts, backward_period(): group_start = jnp.searchsorted(ordered, ordered, side='left')  99.6 us
    all_to_all x1, blocking collectives, backward_period(): lax.all_to_all(outgoing, 'path', split_axis=1, concat_axis=1, tiled=True)  80.1 us
    all_to_all x1, waiting for transfers between devices, backward_period(): lax.all_to_all(outgoing, 'path', split_axis=1, concat_axis=1, tiled=True)  72.1 us
    all_to_all x2, starting transfers between devices, backward_period(): jax.lax.all_to_all(jnp.stack([weight_block] * jax.lax.psum(1, 'path')), '...  25.5 us
    scatter x2, other arithmetic, backward_period(): outgoing.at[:, position].set(jnp.take(regress_rows, ranking, axis=1))  21 us
    all_to_all x2, waiting for transfers between devices, backward_period(): jax.lax.all_to_all(jnp.stack([weight_block] * jax.lax.psum(1, 'path')), '...  19.5 us
  transfers between devices with their start and end apart: 5, of which 5 were waited for; matrix products, arithmetic and copies ran while one was open for 3% of the time, Pallas kernels for 0%

profile of v1, /device:TPU:1, one launch (start us, length us, event | category | flops | bytes accessed | tf_op | source)
XLA Modules:
  0.0 925.9 jit_solution(8350163669753964044)
XLA Ops:
  7.9 6.9 gather_fusion.2
  24.3 50.7 %while.47 = (s32[]{:T(128)}, u32[1024]{0:T(1024)S(1)}, u32[1024]{0:T(1024)S(1)}, s32[1024]{0:T(1024)S(1)}, s32[]{:T(128)}, /*index=5*/s32[]{:T(128)}, s32[]{}) while((s32[]{:T(128)}, u32[1024]{0:T(1024)S(1)}, u32[1024]{0:T(1024)S(1)}, s32[1024]{0:T(1024)S(1)}, s32[]{:T(128)}, /*index=5*/s32[]{:T(128)}, s32[]{}) %tuple.135), condition=%wide.region_3.0_spmd.clone, body=%wide.region_2.5_spmd.clone.sunk | while | flops 19460 | bytes 67685 | solution.py:44
  75.1 6.9 gather_fusion.5
  92.7 50.7 %while.48 = (s32[]{:T(128)}, u32[1024]{0:T(1024)S(1)}, u32[1024]{0:T(1024)S(1)}, s32[1024]{0:T(1024)S(1)}, s32[]{:T(128)}, /*index=5*/s32[]{:T(128)}, s32[]{}) while((s32[]{:T(128)}, u32[1024]{0:T(1024)S(1)}, u32[1024]{0:T(1024)S(1)}, s32[1024]{0:T(1024)S(1)}, s32[]{:T(128)}, /*index=5*/s32[]{:T(128)}, s32[]{}) %tuple.132), condition=%wide.region_16.24_spmd.clone, body=%wide.region_15.23_spmd.clone.sunk | while | flops 19460 | bytes 67685 | solution.py:44
  146.8 10.5 %scatter_custom_fusion = f32[257,2048]{0,1:T(8,128)} fusion(s32[1024]{0:T(1024)S(1)} %get-tuple-element.290, f32[]{:T(128)} %constant.182.clone.1, f32[]{:T(128)} %constant.164.clone.2, pred[1024]{0:T(1024)(128)(4,1)S(1)} %get-tuple-element.260, f32[257,1024]{0,1:T(8,128)S(1)} %copy.82, s32[1024]{0:T(1024)S(1)} %fusion.68), kind=kCustom, calls=%fused_computation.30 | custom fusion | flops 263168 | bytes 3683336 | tf_op jit(solution)/shard_map/scatter | solution.py:52
  157.2 13.0 %all-to-all-start = ((f32[257,64,32]{0,2,1:T(8,128)}), f32[257,64,32]{0,2,1:T(8,128)S(1)}, u32[]{:S(2)}, u32[]{:S(2)}) async-start(f32[257,64,32]{0,2,1:T(8,128)} %bitcast.259), calls=%async_computation | async-start | bytes 6291456 | tf_op jit(solution)/shard_map/all_to_all | solution.py:55
  170.6 72.1 %all-to-all-done = f32[257,64,32]{0,2,1:T(8,128)S(1)} async-done(((f32[257,64,32]{0,2,1:T(8,128)}), f32[257,64,32]{0,2,1:T(8,128)S(1)}, u32[]{:S(2)}, u32[]{:S(2)}) %all-to-all-start) | async-done | bytes 2105376 | tf_op jit(solution)/shard_map/all_to_all | solution.py:55
  268.1 8.3 all-gather.3.cloned.1.call-done
  279.2 47.4 %custom-call.25 = f32[4,128,128]{2,1,0:T(8,128)S(1)} custom-call(f32[4,128,128]{2,1,0:T(8,128)S(1)} %cholesky.198), custom_call_target="Cholesky" | custom-call | tf_op jit(solution)/shard_map/jit(cholesky)/cholesky | solution.py:66
  326.7 39.3 %custom-call.26 = f32[4,1,128,128]{2,3,1,0:T(8,128)S(1)} custom-call(f32[4,1,128,128]{3,2,1,0:T(8,128)S(1)} %select_bitcast_fusion.1), custom_call_target="InvertDiagBlocksLowerTriangular" | custom-call | tf_op jit(solution)/shard_map/jit(cholesky)/cholesky | solution.py:66
  367.1 46.9 %custom-call.27 = f32[4,128,128]{2,1,0:T(8,128)S(1)} custom-call(f32[4,128,128]{2,1,0:T(8,128)S(1)} %convolution_subtract_fusion.1), custom_call_target="Cholesky" | custom-call | tf_op jit(solution)/shard_map/jit(cholesky)/cholesky | solution.py:66
  419.5 78.8 %custom-call.29 = f32[4,2,128,128]{2,3,1,0:T(8,128)S(1)} custom-call(f32[4,2,128,128]{3,2,1,0:T(8,128)S(1)} %bitcast.262), custom_call_target="InvertDiagBlocksLowerTriangular" | custom-call | tf_op jit(solution)/shard_map/triangular_solve/custom-call.4 | solution.py:70
  502.3 12.7 %all-to-all-start.1 = ((f32[64,1,256]{2,1,0:T(1,128)}), f32[64,1,256]{2,1,0:T(1,128)S(1)}, u32[]{:S(2)}, u32[]{:S(2)}) async-start(f32[64,1,256]{2,1,0:T(1,128)} %reshape.419), calls=%async_computation.1 | async-start | bytes 131072 | tf_op jit(solution)/shard_map/all_to_all | solution.py:75
  515.1 10.0 %all-to-all-done.1 = f32[64,1,256]{2,1,0:T(1,128)S(1)} async-done(((f32[64,1,256]{2,1,0:T(1,128)}), f32[64,1,256]{2,1,0:T(1,128)S(1)}, u32[]{:S(2)}, u32[]{:S(2)}) %all-to-all-start.1) | async-done | bytes 65568 | tf_op jit(solution)/shard_map/all_to_all | solution.py:75
  529.8 7.3 psum.14
  537.9 10.6 %scatter_custom_fusion.1 = f32[257,2048]{0,1:T(8,128)} fusion(s32[1024]{0:T(1024)} %get-tuple-element.289, f32[]{:T(128)} %constant.182.clone.1, f32[]{:T(128)} %constant.164.clone.2, pred[1024]{0:T(1024)(128)(4,1)S(1)} %copy-done.22, f32[257,1024]{0,1:T(8,128)S(1)} %copy.92, s32[1024]{0:T(1024)S(1)} %copy-done.14), kind=kCustom, calls=%fused_computation.28 | custom fusion | flops 263168 | bytes 3164160 | tf_op jit(solution)/shard_map/scatter | solution.py:52
  548.5 80.1 %all_to_all.20 = f32[257,64,32]{0,2,1:T(8,128)S(1)} all-to-all(f32[257,64,32]{0,2,1:T(8,128)} %bitcast.260), channel_id=1, replica_groups=mesh['path'=64,'rep'=4] {'path'}, dimensions={1} | all-to-all | bytes 4210688 | tf_op jit(solution)/shard_map/all_to_all | solution.py:55
  662.3 47.3 %custom-call.30 = f32[4,128,128]{2,1,0:T(8,128)S(1)} custom-call(f32[4,128,128]{2,1,0:T(8,128)S(1)} %cholesky.201), custom_call_target="Cholesky" | custom-call | tf_op jit(solution)/shard_map/jit(cholesky)/cholesky | solution.py:66
  709.8 39.3 %custom-call.31 = f32[4,1,128,128]{2,3,1,0:T(8,128)S(1)} custom-call(f32[4,1,128,128]{3,2,1,0:T(8,128)S(1)} %select_bitcast_fusion), custom_call_target="InvertDiagBlocksLowerTriangular" | custom-call | tf_op jit(solution)/shard_map/jit(cholesky)/cholesky | solution.py:66
  750.2 46.9 %custom-call.32 = f32[4,128,128]{2,1,0:T(8,128)S(1)} custom-call(f32[4,128,128]{2,1,0:T(8,128)S(1)} %convolution_subtract_fusion), custom_call_target="Cholesky" | custom-call | tf_op jit(solution)/shard_map/jit(cholesky)/cholesky | solution.py:66
  801.8 78.8 %custom-call.34 = f32[4,2,128,128]{2,3,1,0:T(8,128)S(1)} custom-call(f32[4,2,128,128]{3,2,1,0:T(8,128)S(1)} %bitcast.261), custom_call_target="InvertDiagBlocksLowerTriangular" | custom-call | tf_op jit(solution)/shard_map/triangular_solve/custom-call.4 | solution.py:70
  884.1 12.7 %all-to-all-start.3 = ((f32[64,1,256]{2,1,0:T(1,128)}), f32[64,1,256]{2,1,0:T(1,128)S(1)}, u32[]{:S(2)}, u32[]{:S(2)}) async-start(f32[64,1,256]{2,1,0:T(1,128)} %reshape.421), calls=%async_computation.3 | async-start | bytes 131072 | tf_op jit(solution)/shard_map/all_to_all | solution.py:75
  897.5 9.4 %all-to-all-done.3 = f32[64,1,256]{2,1,0:T(1,128)S(1)} async-done(((f32[64,1,256]{2,1,0:T(1,128)}), f32[64,1,256]{2,1,0:T(1,128)S(1)}, u32[]{:S(2)}, u32[]{:S(2)}) %all-to-all-start.3) | async-done | bytes 65568 | tf_op jit(solution)/shard_map/all_to_all | solution.py:75
  911.0 7.3 psum.15
  (307 shorter events, 225.4 us)
Async XLA Ops:
  7.2 137.4 %copy-start = (f32[223,32]{0,1:T(8,128)S(1)}, f32[223,32]{0,1:T(8,128)}, u32[]{:S(2)}) copy-start(f32[223,32]{0,1:T(8,128)} %param.26) | copy-start | bytes 85636
  92.6 50.7 %copy-start.9 = (f32[32,1024]{1,0:T(8,128)S(1)}, f32[32,1024]{1,0:T(8,128)}, u32[]{:S(2)}) copy-start(f32[32,1024]{1,0:T(8,128)} %param.23) | copy-start | bytes 393220
  92.6 50.7 %copy-start.11 = (f32[2,32,1024]{2,1,0:T(8,128)S(1)}, f32[2,32,1024]{2,1,0:T(8,128)}, u32[]{:S(2)}) copy-start(f32[2,32,1024]{2,1,0:T(8,128)} %param.24) | copy-start | bytes 786436
  92.7 50.7 %copy-start.12 = (f32[32,32]{1,0:T(8,128)S(1)}, f32[32,32]{1,0:T(8,128)}, u32[]{:S(2)}) copy-start(f32[32,32]{1,0:T(8,128)} %param.25) | copy-start | bytes 12292
  144.3 1.2 copy-start.7
  157.2 85.4 %all-to-all-start = ((f32[257,64,32]{0,2,1:T(8,128)}), f32[257,64,32]{0,2,1:T(8,128)S(1)}, u32[]{:S(2)}, u32[]{:S(2)}) async-start(f32[257,64,32]{0,2,1:T(8,128)} %bitcast.259), calls=%async_computation | async-start | bytes 6291456 | tf_op jit(solution)/shard_map/all_to_all | solution.py:55
  170.2 106.2 %all-gather.3.cloned.1.call-start = ((), (), s32[]{:S(2)}) async-start(), calls=%async_computation.4 | async-start | bytes 1310720 | tf_op jit(solution)/shard_map/all_gather | solution.py:63
  367.1 47.4 %copy-start.27 = (s32[2]{0:T(128)S(1)}, s32[2]{0:T(128)}, u32[]{:S(2)}) copy-start(s32[2]{0:T(128)} %iota_multiply_fusion) | copy-start | bytes 28
  414.6 83.6 %copy-start.18 = (f32[4,128,1]{1,0,2:T(4,128)S(1)}, f32[4,128,1]{1,0,2:T(4,128)}, u32[]{:S(2)}) copy-start(f32[4,128,1]{1,0,2:T(4,128)} %slice.172) | copy-start | bytes 6148
  502.3 22.8 %all-to-all-start.1 = ((f32[64,1,256]{2,1,0:T(1,128)}), f32[64,1,256]{2,1,0:T(1,128)S(1)}, u32[]{:S(2)}, u32[]{:S(2)}) async-start(f32[64,1,256]{2,1,0:T(1,128)} %reshape.419), calls=%async_computation.1 | async-start | bytes 131072 | tf_op jit(solution)/shard_map/all_to_all | solution.py:75
  515.0 144.6 %all-gather.5.cloned.1.call-start = ((), (), s32[]{:S(2)}) async-start(), calls=%async_computation.5 | async-start | bytes 1310720 | tf_op jit(solution)/shard_map/all_gather | solution.py:63
  526.6 3.1 copy-start.5
  526.6 3.1 copy-start.8
  526.6 3.1 copy-start.24
  529.4 7.6 copy-start.15
  529.4 7.6 copy-start.4
  635.0 5.8 copy-start.21
  797.6 83.0 %copy-start.17 = (f32[4,128,1]{1,0,2:T(4,128)S(1)}, f32[4,128,1]{1,0,2:T(4,128)}, u32[]{:S(2)}) copy-start(f32[4,128,1]{1,0,2:T(4,128)} %slice.179) | copy-start | bytes 6148
  801.7 95.1 %copy-start.10 = (f32[32,1024]{1,0:T(8,128)S(1)}, f32[32,1024]{1,0:T(8,128)}, u32[]{:S(2)}) copy-start(f32[32,1024]{1,0:T(8,128)} %param.23) | copy-start | bytes 393220
  801.7 95.1 %copy-start.19 = (f32[1,4,64]{2,1,0:T(4,128)S(1)}, f32[1,4,64]{2,1,0:T(4,128)}, u32[]{:S(2)}) copy-start(f32[1,4,64]{2,1,0:T(4,128)} %get-tuple-element.275) | copy-start | bytes 3076
  801.7 106.0 %copy-start.16 = (s32[1024]{0:T(1024)S(1)}, s32[1024]{0:T(1024)}, u32[]{:S(2)}) copy-start(s32[1024]{0:T(1024)} %fusion.72) | copy-start | bytes 12292
  884.1 22.8 %all-to-all-start.3 = ((f32[64,1,256]{2,1,0:T(1,128)}), f32[64,1,256]{2,1,0:T(1,128)S(1)}, u32[]{:S(2)}, u32[]{:S(2)}) async-start(f32[64,1,256]{2,1,0:T(1,128)} %reshape.421), calls=%async_computation.3 | async-start | bytes 131072 | tf_op jit(solution)/shard_map/all_to_all | solution.py:75
  907.8 3.0 copy-start.6
  907.8 3.0 copy-start.23
  (9 other events, 7.0 us)
Sparse Core Ops, SparseCore 0:
  254.3 22.1 all-gather.2
  640.3 19.2 all-gather.4
